TPU v7x, 512 devices: a whole 4x8x8 slice. The times are simulated.
512 devices in a mesh: lat: 16 (over y_hi, x, core), lon: 32 (over z, y_lo).
Axes of the slice: x: 4, y: 8 (y_hi: 2, y_lo: 4; y = y_hi * 4 + y_lo), z: 8, core: 2. Of those that a mesh axis runs over, the one named last changes fastest.
Arguments:
- queries: bfloat16 [131072, 1024], P(('lat', 'lon')), may hold values from -6 to 6
- gain: bfloat16 [1024], replicated, may hold values from 0.099609375 to 1.8984375
- w_query: bfloat16 [1024, 1024], P('lon'), may hold values from -0.1875 to 0.1875
- w_out: bfloat16 [1024, 1024], P(None, 'lon'), may hold values from -0.75 to 0.75
- kv_cache: bfloat16 [2, 32, 256, 1024], P(None, 'lat'), may hold values from -60 to 60
- nbr_lists: int32 [512, 4], P(('lat', 'lon')), may hold values from 0 to 31, as said below
- counts: int32 [512], P(('lat', 'lon')), may hold values from 1 to 4, as said below
Outputs:
- decoded: bfloat16 [131072, 1024], P(('lat', 'lon'))
Inputs may be any that keep to these rules, and one draw needn't show every extreme that they name: `nbr_lists`: query block b lies in band b // 32; band k holds latent blocks k * 2 to (k+1) * 2 - 1. Entries of b's list lie in its band or the bands beside it; its first counts[b] entries differ, the others repeat entry 0. `counts`: query blocks of the first and last band have 4 valid slots.
All inputs are finite; a program needn't handle non-finite values.
Results may differ from a plain program's by a relative error of at most 0.007.
The roundings to bfloat16 on the way count: a program that leaves them out, or rounds other values in their place, can miss the bound.
Values may be sent and summed in bfloat16 or wider, within the bound.
No kernel may reach another device: no remote copies, remote signals or barrier semaphores. Data moves between devices by JAX's collectives and lax.ppermute only.
A program may use at most 64 MiB of HBM per device.

v0:
```python
import jax
import jax.numpy as jnp
from jax import lax
from jax.sharding import PartitionSpec as P

H = 16
HD = 64
BLOCK_TOKENS = 256


def padded(array, sides, width):
    for axis, dim in sides:
        devices, length = (lax.axis_size(axis), array.shape[dim])
        up = [(i, (i + 1) % devices) for i in range(devices - 1)]
        down = [(j, i) for i, j in up]
        last = lax.slice_in_dim(array, length - width, length, axis=dim)
        initial = lax.slice_in_dim(array, 0, width, axis=dim)
        before = lax.ppermute(last, axis, up)
        after = lax.ppermute(initial, axis, down)
        array = jnp.concatenate([before, array, after], axis=dim)
    return array


def on_device(queries, gain, w_query, w_out, kv_cache, nbr_lists, counts):
    rows = queries.astype(jnp.float32)
    rowwise_scale = lax.rsqrt(jnp.mean(rows * rows, axis=1, keepdims=True) + 1e-05)
    normed = (rows * rowwise_scale * gain.astype(jnp.float32)[None, :]).astype(jnp.bfloat16)
    row_count = queries.shape[0]
    query_count = row_count // BLOCK_TOKENS
    projected = jnp.dot(
        normed,
        lax.all_gather(w_query, "lon", axis=0, tiled=True),
        preferred_element_type=jnp.float32,
    )
    query = (projected * HD ** (-0.5)).astype(jnp.bfloat16)
    q_heads = query.reshape(query_count, BLOCK_TOKENS, H, HD)
    lat_index = lax.axis_index("lat")
    blocks_here = kv_cache.shape[1]
    window = padded(kv_cache, (("lat", 1),), blocks_here)
    key_window = window[0].reshape(3 * blocks_here, BLOCK_TOKENS, H, HD)
    value_window = window[1].reshape(3 * blocks_here, BLOCK_TOKENS, H, HD)
    local_lists = nbr_lists - (lat_index - 1) * blocks_here

    def update(state, scores, is_live, value_rows, value_form):
        best, total_sum, running = state
        peak = jnp.max(scores, axis=3)
        new_best = jnp.where(is_live[:, None, None], jnp.maximum(best, peak), best)
        rescale = jnp.exp(best - new_best)
        expo = jnp.where(is_live[:, None, None, None], jnp.exp(scores - new_best[..., None]), 0.0)
        total_sum = total_sum * rescale + jnp.sum(expo, axis=3)
        mixed = jnp.einsum(
            value_form, expo.astype(jnp.bfloat16), value_rows, preferred_element_type=jnp.float32
        )
        running = running * rescale[..., None] + mixed
        return (new_best, total_sum, running)

    start_state = (
        jnp.full((query_count, BLOCK_TOKENS, H), -1e30, jnp.float32),
        jnp.zeros((query_count, BLOCK_TOKENS, H), jnp.float32),
        jnp.zeros((query_count, BLOCK_TOKENS, H, HD), jnp.float32),
    )

    def listed_step(slot_index, state):
        picked = lax.dynamic_slice_in_dim(local_lists, slot_index, 1, 1)[:, 0]
        key_rows = jnp.take(key_window, picked, axis=0)
        value_rows = jnp.take(value_window, picked, axis=0)
        scores = jnp.einsum(
            "bqhd,bkhd->bqhk", q_heads, key_rows, preferred_element_type=jnp.float32
        )
        return update(state, scores, slot_index < counts, value_rows, "bqhk,bkhd->bqhd")

    final_state = lax.fori_loop(0, jnp.max(counts), listed_step, start_state)
    attended = (
        (final_state[2] / final_state[1][..., None]).reshape(row_count, H * HD).astype(jnp.bfloat16)
    )
    decoded = jnp.dot(
        attended,
        lax.all_gather(w_out, "lon", axis=1, tiled=True),
        preferred_element_type=jnp.float32,
    )
    return decoded.astype(jnp.bfloat16)


def solution(mesh):
    placed = (
        P(("lat", "lon"), None),
        P(),
        P("lon", None),
        P(None, "lon"),
        P(None, "lat", None, None),
        P(("lat", "lon"), None),
        P(("lat", "lon")),
    )
    return jax.shard_map(
        on_device, mesh=mesh, in_specs=placed, out_specs=P(("lat", "lon"), None), check_vma=False
    )
```

profile of v0, /device:TPU:6, one launch (start us, length us, event | category | flops | bytes accessed | tf_op | source)
XLA Modules:
  0.0 351.9 jit_solution(9030099862044191392)
XLA Ops:
  6.5 0.0 copy-start
  6.5 0.0 all-gather.3.cloned.1.call-start
  6.5 0.7 all-gather.3.cloned.1.call-update
  7.3 0.0 all-gather.5.cloned.1.call-start
  7.3 1.9 collective-permute-start
  9.2 3.6 %collective-permute-start.1 = (bf16[2,2,256,1024]{3,2,1,0:T(8,128)(2,1)}, bf16[2,2,256,1024]{3,2,1,0:T(8,128)(2,1)}, u32[]{:S(2)}, u32[]{:S(2)}) collective-permute-start(bf16[2,2,256,1024]{3,2,1,0:T(8,128)(2,1)} %param.15), channel_id=1, source_target_pairs={{32,0},{64,32},{96,64},{128,96},{160,128},{192,160},{224,192},{256... | collective-permute-start | bytes 6291464 | tf_op jit(solution)/shard_map/ppermute | solution.py:19
  12.9 0.0 all-gather.5.cloned.1.call-update
  12.9 0.7 convert_element_type.25
  13.6 1.2 fusion.35
  14.8 0.7 broadcast_subtract_fusion
  15.5 19.5 %collective-permute-done = bf16[2,2,256,1024]{3,2,1,0:T(8,128)(2,1)} collective-permute-done((bf16[2,2,256,1024]{3,2,1,0:T(8,128)(2,1)}, bf16[2,2,256,1024]{3,2,1,0:T(8,128)(2,1)}, u32[]{:S(2)}, u32[]{:S(2)}) %collective-permute-start) | collective-permute-done | bytes 2097184 | tf_op jit(solution)/shard_map/ppermute | solution.py:18
  35.0 1.8 constant_dynamic-update-slice_fusion.2
  36.7 0.0 copy-done
  36.7 0.2 constant_dynamic-update-slice_fusion.1
  36.9 0.0 collective-permute-done.1
  36.9 1.8 constant_dynamic-update-slice_fusion
  38.7 2.7 fusion.41
  41.5 4.7 %copy.13 = bf16[1,6,256,1024]{2,3,1,0:T(8,128)(2,1)} copy(bf16[1,6,256,1024]{3,2,1,0:T(8,128)(2,1)} %get-tuple-element.108) | data formatting | bytes 6291456 | tf_op jit(solution)/shard_map/slice | solution.py:40
  46.1 2.8 copy.15
  48.9 131.5 %all-gather.3.cloned.1.call-done = bf16[1024,1024]{1,0:T(8,128)(2,1)} async-done(((bf16[32,1024]{1,0:T(8,128)(2,1)}), bf16[1024,1024]{1,0:T(8,128)(2,1)}) %all-gather.3.cloned.1.call-update) | async-done | bytes 2097168 | tf_op jit(solution)/shard_map/all_gather | solution.py:32
  180.5 2.5 fusion.34
  183.0 0.2 copy.14
  183.2 0.1 broadcast_in_dim.49
  183.4 34.2 %while.15 = (s32[]{:T(128)}, f32[1,256,16]{1,2,0:T(8,128)S(1)}, f32[1,256,16]{1,2,0:T(8,128)S(1)}, f32[1,256,16,64]{1,3,2,0:T(8,128)S(1)}, s32[]{:T(128)}, /*ind...) while((s32[]{:T(128)}, f32[1,256,16]{1,2,0:T(8,128)S(1)}, ...), condition=%wide.region_4.0_spmd, body=%wide.region_1.5_spmd.sunk | while | flops 276840448 | bytes 16517893 | solution.py:72
  184.0 0.6 constant_dynamic-slice_fusion.2
  186.5 1.8 bitcast_reduce_fusion.2
  189.0 2.0 fusion.54
  191.0 0.7 fusion.53
  192.4 0.6 constant_dynamic-slice_fusion.2
  194.9 1.8 bitcast_reduce_fusion.2
  197.4 2.0 fusion.54
  199.4 0.7 fusion.53
  200.8 0.6 constant_dynamic-slice_fusion.2
  203.3 1.8 bitcast_reduce_fusion.2
  205.8 2.0 fusion.54
  207.8 0.7 fusion.53
  209.2 0.6 constant_dynamic-slice_fusion.2
  211.7 1.8 bitcast_reduce_fusion.2
  214.2 2.0 fusion.54
  216.2 0.7 fusion.53
  217.6 0.1 divide_convert_fusion
  217.7 124.2 %all-gather.5.cloned.1.call-done = bf16[1024,1024]{0,1:T(8,128)(2,1)} async-done(((bf16[1024,32]{0,1:T(8,128)(2,1)}), bf16[1024,1024]{0,1:T(8,128)(2,1)}) %all-gather.5.cloned.1.call-update) | async-done | bytes 2097168 | tf_op jit(solution)/shard_map/all_gather | solution.py:78
  341.9 3.1 convolution_convert_fusion
  (15 shorter events, 0.1 us)
Async XLA Ops:
  6.5 30.2 %copy-start = (bf16[2,2,256,1024]{3,2,1,0:T(8,128)(2,1)S(1)}, bf16[2,2,256,1024]{3,2,1,0:T(8,128)(2,1)}, u32[]{:S(2)}) copy-start(bf16[2,2,256,1024]{3,2,1,0:T(8,128)(2,1)} %param.15) | copy-start | bytes 6291460
  6.5 173.9 %all-gather.3.cloned.1.call-start = ((), (), s32[]{:S(2)}) async-start(), calls=%async_computation | async-start | bytes 2162688 | tf_op jit(solution)/shard_map/all_gather | solution.py:32
  7.3 334.7 %all-gather.5.cloned.1.call-start = ((), (), s32[]{:S(2)}) async-start(), calls=%async_computation.1 | async-start | bytes 2162688 | tf_op jit(solution)/shard_map/all_gather | solution.py:78
  7.3 27.7 %collective-permute-start = (bf16[2,2,256,1024]{3,2,1,0:T(8,128)(2,1)}, bf16[2,2,256,1024]{3,2,1,0:T(8,128)(2,1)}, u32[]{:S(2)}, u32[]{:S(2)}) collective-permute-start(bf16[2,2,256,1024]{3,2,1,0:T(8,128)(2,1)} %param.15), channel_id=1, source_target_pairs={{0,32},{32,64},{64,96},{96,128},{128,160},{160,192},{192,224},{224... | collective-permute-start | bytes 6291464 | tf_op jit(solution)/shard_map/ppermute | solution.py:18
  9.2 27.7 %collective-permute-start.1 = (bf16[2,2,256,1024]{3,2,1,0:T(8,128)(2,1)}, bf16[2,2,256,1024]{3,2,1,0:T(8,128)(2,1)}, u32[]{:S(2)}, u32[]{:S(2)}) collective-permute-start(bf16[2,2,256,1024]{3,2,1,0:T(8,128)(2,1)} %param.15), channel_id=1, source_target_pairs={{32,0},{64,32},{96,64},{128,96},{160,128},{192,160},{224,192},{256... | collective-permute-start | bytes 6291464 | tf_op jit(solution)/shard_map/ppermute | solution.py:19
Sparse Core Ops, SparseCore 0:
  9.4 171.0 all-gather.2
  182.6 159.3 all-gather.4
where the time goes:
time: 353 us; the launch traced here: 352 us
  waiting for transfers between devices  276 us (78%)
  matrix products  20.8 us (6%)
  local copies, waits for them, and re-layouts  16.8 us (5%)
  loops' own time  13.6 us (4%)
  between operations  13.5 us (4%)
  other arithmetic  5.63 us (2%)
  starting transfers between devices  5.6 us (2%)
    all_gather x1, waiting for transfers between devices, on_device(): lax.all_gather(w_query, 'lon', axis=0, tiled=True)  132 us
    all_gather x1, waiting for transfers between devices, on_device(): lax.all_gather(w_out, 'lon', axis=1, tiled=True)  124 us
    ppermute x1, waiting for transfers between devices, padded(): before = lax.ppermute(last, axis, up)  19.5 us
    another operation x1, loops' own time, on_device(): final_state = lax.fori_loop(0, jnp.max(counts), listed_step, start_state)  13.6 us
    dot_general x4, matrix products, update(): jnp.einsum(value_form, expo.astype(jnp.bfloat16), value_rows, preferred_e...  7.88 us
    dot_general x4, matrix products, listed_step(): jnp.einsum('bqhd,bkhd->bqhk', q_heads, key_rows, preferred_element_type=j...  7.23 us
  transfers between devices with their start and end apart: 4, of which 3 were waited for; matrix products, arithmetic and copies ran while one was open for 11% of the time, Pallas kernels for 0%

commit v1 on v0

--- a/solution.py
+++ b/solution.py
@@ -29,7 +29,12 @@
     query_count = row_count // BLOCK_TOKENS
     projected = jnp.dot(
         normed,
-        lax.all_gather(w_query, "lon", axis=0, tiled=True),
+        jnp.concatenate(
+            lax.all_to_all(
+                jnp.stack([w_query for _ in range(lax.axis_size("lon"))], axis=0), "lon", 0, 0
+            ),
+            axis=0,
+        ),
         preferred_element_type=jnp.float32,
     )
     query = (projected * HD ** (-0.5)).astype(jnp.bfloat16)

time: 353 us -> 221 us (0.63)
  waiting for transfers between devices: 276 us -> 128 us
  starting transfers between devices: 5.6 us -> 19.5 us
    all_gather x1 -> x0, waiting for transfers between devices: 132 us -> none  [on_device(): lax.all_gather(w_query, 'lon', axis=0, tiled=True)]
    all_gather x1, waiting for transfers between devices: 124 us -> 62.1 us  [on_device(): lax.all_gather(w_out, 'lon', axis=1, tiled=True)]
    all_to_all x0 -> x1, waiting for transfers between devices: none -> 43.9 us  [on_device(): lax.all_to_all(jnp.stack([w_query for _ in range(lax.axis_size('lon'))],...]
    all_to_all x0 -> x1, starting transfers between devices: none -> 13.9 us  [on_device(): lax.all_to_all(jnp.stack([w_query for _ in range(lax.axis_size('lon'))],...]
  transfers between devices with their start and end apart: 4 -> 4, of which waited for: 3 -> 3; matrix products, arithmetic and copies ran while one was open for 11% -> 17% of each run, Pallas kernels for 0% -> 0%
where the time goes in v1:
time: 221 us; the launch traced here: 218 us
  waiting for transfers between devices  128 us (58%)
  matrix products  20.8 us (9%)
  starting transfers between devices  19.5 us (9%)
  local copies, waits for them, and re-layouts  19.4 us (9%)
  loops' own time  14.2 us (6%)
  between operations  13.5 us (6%)
  other arithmetic  3.25 us (1%)
    all_gather x1, waiting for transfers between devices, on_device(): lax.all_gather(w_out, 'lon', axis=1, tiled=True)  62.1 us
    all_to_all x1, waiting for transfers between devices, on_device(): lax.all_to_all(jnp.stack([w_query for _ in range(lax.axis_size('lon'))],...  43.9 us
    ppermute x1, waiting for transfers between devices, padded(): before = lax.ppermute(last, axis, up)  21.6 us
    another operation x1, loops' own time, on_device(): final_state = lax.fori_loop(0, jnp.max(counts), listed_step, start_state)  14.2 us
    all_to_all x1, starting transfers between devices, on_device(): lax.all_to_all(jnp.stack([w_query for _ in range(lax.axis_size('lon'))],...  13.9 us
    dot_general x4, matrix products, update(): jnp.einsum(value_form, expo.astype(jnp.bfloat16), value_rows, preferred_e...  7.88 us
    dot_general x4, matrix products, listed_step(): jnp.einsum('bqhd,bkhd->bqhk', q_heads, key_rows, preferred_element_type=j...  7.25 us
    slice x2, local copies, waits for them, and re-layouts, on_device(): value_window = window[1].reshape(3 * blocks_here, BLOCK_TOKENS, H, HD)  5.54 us
  transfers between devices with their start and end apart: 4, of which 3 were waited for; matrix products, arithmetic and copies ran while one was open for 17% of the time, Pallas kernels for 0%

profile of v1, /device:TPU:6, one launch (start us, length us, event | category | flops | bytes accessed | tf_op | source)
XLA Modules:
  0.0 218.4 jit_solution(8846543718287634392)
XLA Ops:
  6.5 0.0 copy-start
  6.5 0.0 copy-start.2
  6.5 0.0 copy-start.1
  6.5 0.0 copy-start.3
  6.5 2.6 %stack.2 = bf16[32,32,1024]{2,1,0:T(8,128)(2,1)} broadcast(bf16[32,1024]{1,0:T(8,128)(2,1)} %param.13), dimensions={1,2} | broadcast | bytes 2162688 | tf_op jit(solution)/shard_map/stack | solution.py:34
  9.1 13.9 %all-to-all-start = ((bf16[32,32,1024]{2,1,0:T(8,128)(2,1)}), bf16[32,32,1024]{2,1,0:T(8,128)(2,1)}, u32[]{:S(2)}, u32[]{:S(2)}) async-start(bf16[32,32,1024]{2,1,0:T(8,128)(2,1)} %stack.2), calls=%async_computation | async-start | bytes 4194304 | tf_op jit(solution)/shard_map/all_to_all | solution.py:33
  23.0 0.0 all-gather.2.cloned.1.call-start
  23.1 0.0 copy-done
  23.1 1.9 collective-permute-start
  25.0 3.6 %collective-permute-start.1 = (bf16[2,2,256,1024]{3,2,1,0:T(8,128)(2,1)S(1)}, bf16[2,2,256,1024]{3,2,1,0:T(8,128)(2,1)}, u32[]{:S(2)}, u32[]{:S(2)}) collective-permute-start(bf16[2,2,256,1024]{3,2,1,0:T(8,128)(2,1)S(1)} %copy-done), channel_id=1, source_target_pairs={{32,0},{64,32},{96,64},{128,96},{160,128},{192,160},{224,192},{256... | collective-permute-start | bytes 6291464 | tf_op jit(solution)/shard_map/ppermute | solution.py:19
  28.6 0.0 all-gather.2.cloned.1.call-update
  28.7 0.0 copy-done.2
  28.7 0.0 copy-done.1
  28.7 0.2 fusion.35
  28.9 0.0 copy-done.3
  28.9 21.6 %collective-permute-done = bf16[2,2,256,1024]{3,2,1,0:T(8,128)(2,1)} collective-permute-done((bf16[2,2,256,1024]{3,2,1,0:T(8,128)(2,1)S(1)}, bf16[2,2,256,1024]{3,2,1,0:T(8,128)(2,1)}, u32[]{:S(2)}, u32[]{:S(2)}) %collective-permute-start) | collective-permute-done | bytes 2097184 | tf_op jit(solution)/shard_map/ppermute | solution.py:18
  50.5 1.8 constant_dynamic-update-slice_fusion.2
  52.3 0.2 constant_dynamic-update-slice_fusion.1
  52.5 0.0 collective-permute-done.1
  52.5 1.8 constant_dynamic-update-slice_fusion
  54.3 2.7 %fusion.41 = (bf16[1,6,256,1024]{3,2,1,0:T(8,128)(2,1)S(1)}, bf16[1,6,256,1024]{3,2,1,0:T(8,128)(2,1)}) fusion(bf16[2,6,256,1024]{3,2,1,0:T(8,128)(2,1)S(1)} %constant_dynamic-update-slice_fusion), kind=kLoop, calls=%fused_computation.51 | loop fusion | bytes 12582912 | tf_op jit(solution)/shard_map/slice | solution.py:46
  57.0 4.7 %copy.13 = bf16[1,6,256,1024]{2,3,1,0:T(8,128)(2,1)} copy(bf16[1,6,256,1024]{3,2,1,0:T(8,128)(2,1)} %get-tuple-element.108) | data formatting | bytes 6291456 | tf_op jit(solution)/shard_map/slice | solution.py:45
  61.7 2.8 %copy.15 = bf16[1,6,256,1024]{2,3,1,0:T(8,128)(2,1)} copy(bf16[1,6,256,1024]{3,2,1,0:T(8,128)(2,1)S(1)} %get-tuple-element.107) | data formatting | bytes 6291456 | tf_op jit(solution)/shard_map/slice | solution.py:46
  64.5 43.9 %all-to-all-done = bf16[32,32,1024]{2,1,0:T(8,128)(2,1)} async-done(((bf16[32,32,1024]{2,1,0:T(8,128)(2,1)}), bf16[32,32,1024]{2,1,0:T(8,128)(2,1)}, u32[]{:S(2)}, u32[]{:S(2)}) %all-to-all-start) | async-done | bytes 2097184 | tf_op jit(solution)/shard_map/all_to_all | solution.py:33
  108.3 2.5 %fusion.34 = bf16[256,1024]{1,0:T(8,128)(2,1)S(1)} fusion(bf16[1024,1024]{1,0:T(8,128)(2,1)} %bitcast.22, bf16[256,1024]{1,0:T(8,128)(2,1)} %param.11, f32[1024]{0:T(1024)S(1)} %convert_element_type.25, f32[256]{0:T(256)S(1)} %add_rsqrt_fusion), kind=kOutput, calls=%fused_computation.39 | convolution fusion | flops 538443776 | bytes 3150848 | tf_op jit(solution)/shard_map/dot_general | solution.py:30
  110.9 0.2 copy.14
  111.1 0.1 broadcast_in_dim.49
  111.2 34.9 %while.15 = (s32[]{:T(128)}, f32[1,256,16]{1,2,0:T(8,128)S(1)}, f32[1,256,16]{1,2,0:T(8,128)S(1)}, f32[1,256,16,64]{1,3,2,0:T(8,128)S(1)}, s32[]{:T(128)}, /*ind...) while((s32[]{:T(128)}, f32[1,256,16]{1,2,0:T(8,128)S(1)}, ...), condition=%wide.region_4.0_spmd, body=%wide.region_1.5_spmd.sunk | while | flops 276840448 | bytes 16517893 | solution.py:77
  111.9 0.6 constant_dynamic-slice_fusion.2
  114.6 1.8 bitcast_reduce_fusion.2
  117.0 2.0 fusion.54
  119.0 0.7 fusion.53
  120.4 0.6 constant_dynamic-slice_fusion.2
  123.1 1.8 bitcast_reduce_fusion.2
  125.6 2.0 fusion.54
  127.6 0.7 fusion.53
  129.0 0.6 constant_dynamic-slice_fusion.2
  131.7 1.8 bitcast_reduce_fusion.2
  134.2 2.0 fusion.54
  136.2 0.7 fusion.53
  137.6 0.6 constant_dynamic-slice_fusion.2
  140.3 1.8 bitcast_reduce_fusion.2
  142.7 2.0 fusion.54
  144.7 0.7 fusion.53
  146.1 0.1 divide_convert_fusion
  146.2 62.1 %all-gather.2.cloned.1.call-done = bf16[1024,1024]{0,1:T(8,128)(2,1)} async-done(((bf16[1024,32]{0,1:T(8,128)(2,1)}), bf16[1024,1024]{0,1:T(8,128)(2,1)}) %all-gather.2.cloned.1.call-update) | async-done | bytes 2097168 | tf_op jit(solution)/shard_map/all_gather | solution.py:83
  208.4 3.1 %convolution_convert_fusion = bf16[256,1024]{1,0:T(8,128)(2,1)} fusion(bf16[256,1024]{0,1:T(8,128)(2,1)S(1)} %bitcast.109, bf16[1024,1024]{0,1:T(8,128)(2,1)} %all-gather.2.cloned.1.call-done), kind=kOutput, calls=%fused_computation.38 | convolution fusion | flops 537133056 | bytes 3145728 | tf_op jit(solution)/shard_map/dot_general | solution.py:81
  (17 shorter events, 0.1 us)
Async XLA Ops:
  6.5 16.5 %copy-start = (bf16[2,2,256,1024]{3,2,1,0:T(8,128)(2,1)S(1)}, bf16[2,2,256,1024]{3,2,1,0:T(8,128)(2,1)}, u32[]{:S(2)}) copy-start(bf16[2,2,256,1024]{3,2,1,0:T(8,128)(2,1)} %param.15) | copy-start | bytes 6291460
  6.5 22.1 %copy-start.2 = (bf16[1024]{0:T(1024)(128)(2,1)S(1)}, bf16[1024]{0:T(1024)(128)(2,1)}, u32[]{:S(2)}) copy-start(bf16[1024]{0:T(1024)(128)(2,1)} %param.12) | copy-start | bytes 6148
  6.5 22.2 %copy-start.1 = (bf16[256,1024]{1,0:T(8,128)(2,1)S(1)}, bf16[256,1024]{1,0:T(8,128)(2,1)}, u32[]{:S(2)}) copy-start(bf16[256,1024]{1,0:T(8,128)(2,1)} %param.11) | copy-start | bytes 1572868
  6.5 22.4 %copy-start.3 = (s32[1,4]{1,0:T(1,128)S(1)}, s32[1,4]{1,0:T(1,128)}, u32[]{:S(2)}) copy-start(s32[1,4]{1,0:T(1,128)} %param.16) | copy-start | bytes 52
  9.1 99.2 %all-to-all-start = ((bf16[32,32,1024]{2,1,0:T(8,128)(2,1)}), bf16[32,32,1024]{2,1,0:T(8,128)(2,1)}, u32[]{:S(2)}, u32[]{:S(2)}) async-start(bf16[32,32,1024]{2,1,0:T(8,128)(2,1)} %stack.2), calls=%async_computation | async-start | bytes 4194304 | tf_op jit(solution)/shard_map/all_to_all | solution.py:33
  23.0 185.4 %all-gather.2.cloned.1.call-start = ((), (), s32[]{:S(2)}) async-start(), calls=%async_computation.1 | async-start | bytes 2162688 | tf_op jit(solution)/shard_map/all_gather | solution.py:83
  23.1 27.5 %collective-permute-start = (bf16[2,2,256,1024]{3,2,1,0:T(8,128)(2,1)S(1)}, bf16[2,2,256,1024]{3,2,1,0:T(8,128)(2,1)}, u32[]{:S(2)}, u32[]{:S(2)}) collective-permute-start(bf16[2,2,256,1024]{3,2,1,0:T(8,128)(2,1)S(1)} %copy-done), channel_id=1, source_target_pairs={{0,32},{32,64},{64,96},{96,128},{128,160},{160,192},{192,224},{224... | collective-permute-start | bytes 6291464 | tf_op jit(solution)/shard_map/ppermute | solution.py:18
  25.0 27.5 %collective-permute-start.1 = (bf16[2,2,256,1024]{3,2,1,0:T(8,128)(2,1)S(1)}, bf16[2,2,256,1024]{3,2,1,0:T(8,128)(2,1)}, u32[]{:S(2)}, u32[]{:S(2)}) collective-permute-start(bf16[2,2,256,1024]{3,2,1,0:T(8,128)(2,1)S(1)} %copy-done), channel_id=1, source_target_pairs={{32,0},{64,32},{96,64},{128,96},{160,128},{192,160},{224,192},{256... | collective-permute-start | bytes 6291464 | tf_op jit(solution)/shard_map/ppermute | solution.py:19
Sparse Core Ops, SparseCore 0:
  28.8 179.5 all-gather.1
